TPU v7x, 32 devices: a whole 2x2x4 slice. The times are simulated.
32 devices in a mesh: groups: 2 (over y), ctx: 4 (over z), head: 4 (over x, core).
Axes of the slice: x: 2, y: 2, z: 4, core: 2. Of those that a mesh axis runs over, the one named last changes fastest.
Arguments:
- hidden_in: bfloat16 [2048, 4096], P(('groups', 'ctx'), 'head'), parts along dimension 0, may hold values from -6 to 6
- norm_gain: bfloat16 [4096], P('head'), may hold values from 0.099609375 to 1.8984375
- w_query: bfloat16 [4096, 2048], P('ctx', 'head'), may hold values from -8 to 8
- w_key: bfloat16 [4096, 512], P('ctx', 'head'), may hold values from -8 to 8
- w_value: bfloat16 [4096, 512], P('ctx', 'head'), may hold values from -0.09375 to 0.09375
- w_out: bfloat16 [2048, 4096], P('head', 'ctx'), may hold values from -3 to 3
- session_ids: int32 [2048], P('groups'), parts along dimension 0, may hold values from 0 to 3, never falling along the last dimension, each value on 1 to 512 neighbouring positions
- block_anchor: int32 [16], P('groups'), parts along dimension 0, may hold values from 0 to 7, each once
Outputs:
- block_update: bfloat16 [2048, 4096], P(('groups', 'ctx'), 'head'), parts along dimension 0
There are 2 independent parts, one for each index of `groups`. A program takes and returns all parts, laid end to end along the dimension named above; an argument that names none is the same for every part. Nothing has to cross between parts.
Inputs may be any that keep to these rules, and one draw needn't show every extreme that they name: `session_ids`: session numbers never fall along the contiguous order; 4 sessions, each of 1 to 512 tokens, one of exactly 512. `block_anchor`: each of the 8 blocks appears once.
All inputs are finite; a program needn't handle non-finite values.
Results may differ from a plain program's by a relative error of at most 0.0095.
The roundings to bfloat16 on the way count: a program that leaves them out, or rounds other values in their place, can miss the bound.
Values may be sent and summed in bfloat16 or wider, within the bound.
No kernel may reach another device: no remote copies, remote signals or barrier semaphores. Data moves between devices by JAX's collectives and lax.ppermute only.
A program may use at most 64 MiB of HBM per device.

v0:
```python
import math
import jax
import jax.numpy as jnp
from jax import lax
from jax.sharding import PartitionSpec as P

HD = 128
GROUP = 4
BLOCK = 128
norm_epsilon = 1e-05
rotary_base = 500000.0
masked_score = -1e30


def passed_along(block, axis, distance):
    devices = range(lax.axis_size(axis))
    route = [((i - distance) % len(devices), i) for i in devices]
    return lax.ppermute(block, axis, route)


def session_starts(session_ids):
    length = session_ids.shape[0]
    indices = jnp.arange(length, dtype=jnp.int32)
    fresh = jnp.concatenate([jnp.ones((1,), dtype=jnp.bool_), session_ids[1:] != session_ids[:-1]])
    return lax.cummax(jnp.where(fresh, indices, 0), axis=0)


def rotary(vectors, position):
    half_dim = vectors.shape[-1] // 2
    ladder = jnp.arange(half_dim, dtype=jnp.float32) * (2.0 / vectors.shape[-1])
    frequency = jnp.exp(-ladder * math.log(rotary_base))
    angles = position.astype(jnp.float32).reshape((-1,) + (1,) * (vectors.ndim - 1)) * frequency
    cosine = jnp.cos(angles)
    sines = jnp.sin(angles)
    first_half = vectors[..., :half_dim]
    second_half = vectors[..., half_dim:]
    return jnp.concatenate(
        [first_half * cosine - second_half * sines, second_half * cosine + first_half * sines],
        axis=-1,
    )


def attend_core(
    carry_state, query_heads, query_pos, query_seg, key_heads, value_heads, key_pos, key_seg
):
    row_max, row_sum, mixed_sum = carry_state
    scores = jnp.einsum(
        "qagd,kad->qagk", query_heads, key_heads, preferred_element_type=jnp.float32
    ) * (1.0 / math.sqrt(query_heads.shape[-1]))
    allowed = ((query_seg[:, None] == key_seg[None, :]) & (key_pos[None, :] <= query_pos[:, None]))[
        :, None, None, :
    ]
    new_max = jnp.maximum(row_max, jnp.max(jnp.where(allowed, scores, masked_score), axis=-1))
    weights = jnp.where(allowed, jnp.exp(scores - new_max[..., None]), 0.0)
    rescale = jnp.exp(row_max - new_max)
    row_sum = row_sum * rescale + jnp.sum(weights, axis=-1)
    mixed_sum = mixed_sum * rescale[..., None] + jnp.einsum(
        "qagk,kad->qagd",
        weights.astype(jnp.bfloat16),
        value_heads,
        preferred_element_type=jnp.float32,
    )
    return (new_max, row_sum, mixed_sum)


def per_device(hidden_in, norm_gain, w_query, w_key, w_value, w_out, session_ids, block_anchor):
    whole, gain_full = (
        lax.all_gather(hidden_in, "head", axis=1, tiled=True),
        lax.all_gather(norm_gain, "head", axis=0, tiled=True),
    )
    tok_rows = whole.shape[0]
    cycle_size = lax.axis_size("ctx")
    cycle_index = lax.axis_index("ctx")
    per_shard = tok_rows // BLOCK
    starts = session_starts(session_ids)
    seg_table = session_ids.reshape(-1, BLOCK)
    start_table = starts.reshape(-1, BLOCK)
    offsets = jnp.arange(BLOCK, dtype=jnp.int32)

    def token_info(owner):
        blocks_here = lax.dynamic_slice_in_dim(block_anchor, owner * per_shard, per_shard)
        contiguous = (blocks_here[:, None] * BLOCK + offsets[None, :]).reshape(-1)
        session = jnp.take(seg_table, blocks_here, axis=0).reshape(-1)
        position = contiguous - jnp.take(start_table, blocks_here, axis=0).reshape(-1)
        return (contiguous, session, position)

    wide = whole.astype(jnp.float32)
    normed = (
        wide
        * lax.rsqrt(jnp.mean(wide * wide, axis=-1, keepdims=True) + norm_epsilon)
        * gain_full.astype(jnp.float32)
    ).astype(jnp.bfloat16)
    key_cols = w_key.shape[1]
    kv_local = key_cols // HD
    pieces = (
        lax.all_gather(w_query, "ctx", axis=0, tiled=True),
        lax.all_gather(w_key, "ctx", axis=0, tiled=True),
        lax.all_gather(w_value, "ctx", axis=0, tiled=True),
    )
    query_raw, key_raw, value_raw = tuple(
        (jnp.dot(normed, weight_rows, preferred_element_type=jnp.float32) for weight_rows in pieces)
    )
    my_pos, my_seg, my_place = token_info(cycle_index)
    query_heads = rotary(query_raw.reshape(tok_rows, kv_local, GROUP, HD), my_place).astype(
        jnp.bfloat16
    )
    key_heads = rotary(key_raw.reshape(tok_rows, kv_local, HD), my_place).astype(jnp.bfloat16)
    value_heads = value_raw.astype(jnp.bfloat16).reshape(tok_rows, kv_local, HD)

    def attend(current_state, kv_stack, source):
        key_pos, key_seg, unused_place = token_info(source)
        return attend_core(
            current_state, query_heads, my_pos, my_seg, kv_stack[0], kv_stack[1], key_pos, key_seg
        )

    carry_state = (
        jnp.full((tok_rows, kv_local, GROUP), masked_score, jnp.float32),
        jnp.zeros((tok_rows, kv_local, GROUP), jnp.float32),
        jnp.zeros((tok_rows, kv_local, GROUP, HD), jnp.float32),
    )
    own_stack = jnp.stack([key_heads, value_heads])
    carry_state = attend(carry_state, own_stack, cycle_index)

    def cycle_turn(turn_index, loop_carry):
        current_state, moving = loop_carry
        moving = passed_along(moving, "ctx", 1)
        current_state = attend(current_state, moving, (cycle_index - turn_index) % cycle_size)
        return (current_state, moving)

    carry_state, unused_stack = lax.fori_loop(1, cycle_size, cycle_turn, (carry_state, own_stack))
    final_max, row_sum, mixed_sum = carry_state
    attended = (mixed_sum / row_sum[..., None]).astype(jnp.bfloat16).reshape(tok_rows, -1)
    terms = jnp.dot(
        attended,
        lax.all_gather(w_out, "ctx", axis=1, tiled=True),
        preferred_element_type=jnp.float32,
    )
    return lax.psum_scatter(terms.astype(jnp.bfloat16), "head", scatter_dimension=1, tiled=True)


def solution(mesh):
    in_specs = (
        P(("groups", "ctx"), "head"),
        P("head"),
        P("ctx", "head"),
        P("ctx", "head"),
        P("ctx", "head"),
        P("head", "ctx"),
        P("groups"),
        P("groups"),
    )
    out_specs = P(("groups", "ctx"), "head")
    return jax.shard_map(
        per_device, mesh=mesh, in_specs=in_specs, out_specs=out_specs, check_vma=False
    )
```

profile of v0, /device:TPU:0, one launch (start us, length us, event | category | flops | bytes accessed | tf_op | source)
XLA Modules:
  0.0 302.0 jit_solution(423023249203372490)
XLA Ops:
  6.5 0.7 all-gather.6.cloned.1.call-update
  7.3 0.7 all-gather.8.cloned.1.call-update
  8.1 0.7 all-gather.12.cloned.1.call-update
  10.0 0.7 broadcast_multiply_fusion.1
  10.7 0.7 compare_and_fusion.3
  11.4 0.8 slice_compare_fusion
  12.3 1.2 gather_fusion.1
  13.7 6.3 %all_gather.19 = bf16[4096]{0:T(1024)(128)(2,1)S(1)} all-gather(bf16[1024]{0:T(1024)(128)(2,1)} %param.13), channel_id=1, replica_groups=mesh['groups'=2,'ctx'=4,'head'=4] {'head'}, dimensions={0}, use_global_device_ids=true | all-gather | bytes 10240 | tf_op jit(solution)/shard_map/all_gather | solution.py:69
  20.7 0.6 gather_fusion.2
  22.0 12.2 %all-gather.6.cloned.1.call-done = bf16[256,4096]{1,0:T(8,128)(2,1)} async-done(((bf16[256,1024]{1,0:T(8,128)(2,1)}), bf16[256,4096]{1,0:T(8,128)(2,1)}) %all-gather.6.cloned.1.call-update) | async-done | bytes 2097168 | tf_op jit(solution)/shard_map/all_gather | solution.py:68
  34.2 2.2 fusion.17
  36.5 27.3 %all-gather.8.cloned.1.call-done = bf16[4096,128]{1,0:T(8,128)(2,1)} async-done(((bf16[1024,128]{1,0:T(8,128)(2,1)}), bf16[4096,128]{1,0:T(8,128)(2,1)}) %all-gather.8.cloned.1.call-update) | async-done | bytes 1048592 | tf_op jit(solution)/shard_map/all_gather | solution.py:97
  63.8 2.8 convolution_bitcast_fusion.2
  66.9 25.8 %all-gather.12.cloned.1.call-done = bf16[4096,128]{1,0:T(8,128)(2,1)} async-done(((bf16[1024,128]{1,0:T(8,128)(2,1)}), bf16[4096,128]{1,0:T(8,128)(2,1)}) %all-gather.12.cloned.1.call-update) | async-done | bytes 1048592 | tf_op jit(solution)/shard_map/all_gather | solution.py:98
  92.8 2.2 convolution_convert_fusion.1
  95.1 79.2 %all-gather.10.cloned.1.call-done = bf16[4096,512]{1,0:T(8,128)(2,1)} async-done(((bf16[1024,512]{1,0:T(8,128)(2,1)}), bf16[4096,512]{1,0:T(8,128)(2,1)}) %all-gather.10.cloned.1.call-update) | async-done | bytes 4194320 | tf_op jit(solution)/shard_map/all_gather | solution.py:96
  174.4 3.5 %fusion.49 = f32[256,512]{1,0:T(8,128)S(1)} fusion(bf16[4096,512]{1,0:T(8,128)(2,1)} %all-gather.10.cloned.1.call-done, bf16[256,4096]{1,0:T(8,128)(2,1)S(1)} %copy-done, f32[4096]{0:T(1024)S(1)} %convert_element_type.65, f32[256]{0:T(256)S(1)} %add_rsqrt_fusion), kind=kOutput, calls=%fused_computation.101 | convolution fusion | flops 1077936128 | bytes 6833152 | tf_op jit(solution)/shard_map/dot_general | solution.py:101
  179.9 30.9 %while.22 = (s32[]{:T(128)}, f32[256,1,4]{0,2,1:T(4,128)S(1)}, f32[256,1,4]{0,2,1:T(4,128)S(1)}, f32[256,1,4,128]{3,0,2,1:T(8,128)S(1)}, bf16[2,256,1,128]{3,1,2...) while((s32[]{:T(128)}, f32[256,1,4]{0,2,1:T(4,128)S(1)}, ...), condition=%wide.region_8.10_spmd.clone, body=%wide.region_5.9_spmd.clone.sunk | while | flops 137040672 | bytes 5716408 | solution.py:130
  181.1 6.0 %collective-permute-done = bf16[2,256,1,128]{3,1,2,0:T(8,128)(2,1)S(1)} collective-permute-done((bf16[2,256,1,128]{3,1,2,0:T(8,128)(2,1)S(1)}, bf16[2,256,1,128]{3,1,2,0:T(8,128)(2,1)S(1)}, u32[]{:S(2)}, u32[]{:S(2)}) %collective-permute-start) | collective-permute-done | bytes 131104 | tf_op jit(solution)/shard_map/while/body/eval_jaxpr/ppermute | solution.py:18
  189.2 9.2 %collective-permute-done = bf16[2,256,1,128]{3,1,2,0:T(8,128)(2,1)S(1)} collective-permute-done((bf16[2,256,1,128]{3,1,2,0:T(8,128)(2,1)S(1)}, bf16[2,256,1,128]{3,1,2,0:T(8,128)(2,1)S(1)}, u32[]{:S(2)}, u32[]{:S(2)}) %collective-permute-start) | collective-permute-done | bytes 131104 | tf_op jit(solution)/shard_map/while/body/eval_jaxpr/ppermute | solution.py:18
  200.7 9.0 %collective-permute-done = bf16[2,256,1,128]{3,1,2,0:T(8,128)(2,1)S(1)} collective-permute-done((bf16[2,256,1,128]{3,1,2,0:T(8,128)(2,1)S(1)}, bf16[2,256,1,128]{3,1,2,0:T(8,128)(2,1)S(1)}, u32[]{:S(2)}, u32[]{:S(2)}) %collective-permute-start) | collective-permute-done | bytes 131104 | tf_op jit(solution)/shard_map/while/body/eval_jaxpr/ppermute | solution.py:18
  211.1 49.6 %all-gather.14.cloned.1.call-done = bf16[512,4096]{1,0:T(8,128)(2,1)} async-done(((bf16[512,1024]{1,0:T(8,128)(2,1)}), bf16[512,4096]{1,0:T(8,128)(2,1)}) %all-gather.14.cloned.1.call-update) | async-done | bytes 4194320 | tf_op jit(solution)/shard_map/all_gather | solution.py:135
  260.7 4.8 %convolution_convert_fusion = bf16[256,4096]{1,0:T(8,128)(2,1)} fusion(bf16[256,512]{0,1:T(8,128)(2,1)S(1)} %bitcast.132, bf16[512,4096]{1,0:T(8,128)(2,1)} %all-gather.14.cloned.1.call-done), kind=kOutput, calls=%fused_computation.36 | convolution fusion | flops 1074790400 | bytes 6553600 | tf_op jit(solution)/shard_map/dot_general | solution.py:133
  265.5 29.7 %reduce-scatter.2.cloned.1.call-done = bf16[256,1024]{1,0:T(8,128)(2,1)} async-done(((bf16[256,4096]{1,0:T(8,128)(2,1)}), bf16[256,1024]{1,0:T(8,128)(2,1)}) %reduce-scatter.2.cloned.1.call-update) | async-done | bytes 524304 | tf_op jit(solution)/shard_map/reduce_scatter | solution.py:138
  (91 shorter events, 12.1 us)
Async XLA Ops:
  6.5 27.7 %all-gather.6.cloned.1.call-start = ((), (), s32[]{:S(2)}) async-start(), calls=%async_computation.1 | async-start | bytes 2621440 | tf_op jit(solution)/shard_map/all_gather | solution.py:68
  7.3 56.5 %all-gather.8.cloned.1.call-start = ((), (), s32[]{:S(2)}) async-start(), calls=%async_computation.2 | async-start | bytes 1310720 | tf_op jit(solution)/shard_map/all_gather | solution.py:97
  8.0 84.8 %all-gather.12.cloned.1.call-start = ((), (), s32[]{:S(2)}) async-start(), calls=%async_computation.4 | async-start | bytes 1310720 | tf_op jit(solution)/shard_map/all_gather | solution.py:98
  8.7 165.6 %all-gather.10.cloned.1.call-start = ((), (), s32[]{:S(2)}) async-start(), calls=%async_computation.3 | async-start | bytes 5242880 | tf_op jit(solution)/shard_map/all_gather | solution.py:96
  9.3 251.4 %all-gather.14.cloned.1.call-start = ((), (), s32[]{:S(2)}) async-start(), calls=%async_computation.5 | async-start | bytes 5242880 | tf_op jit(solution)/shard_map/all_gather | solution.py:135
  9.9 285.3 %reduce-scatter.2.cloned.1.call-start = ((), (), s32[]{:S(2)}) async-start(), calls=%async_computation.6 | async-start | bytes 2621440 | tf_op jit(solution)/shard_map/reduce_scatter | solution.py:138
  34.2 58.6 %copy-start = (bf16[256,4096]{1,0:T(8,128)(2,1)S(1)}, bf16[256,4096]{1,0:T(8,128)(2,1)}, u32[]{:S(2)}) copy-start(bf16[256,4096]{1,0:T(8,128)(2,1)} %all-gather.6.cloned.1.call-done) | copy-start | bytes 6291460
  178.4 1.6 copy-start.1
  178.4 1.6 copy-start.2
  179.9 7.1 %collective-permute-start = (bf16[2,256,1,128]{3,1,2,0:T(8,128)(2,1)S(1)}, bf16[2,256,1,128]{3,1,2,0:T(8,128)(2,1)S(1)}, u32[]{:S(2)}, u32[]{:S(2)}) collective-permute-start(bf16[2,256,1,128]{3,1,2,0:T(8,128)(2,1)S(1)} %get-tuple-element.504), channel_id=1, source_target_pairs={{12,0},{0,4},{4,8},{8,12},{13,1},{1,5},{5,9},{9,13},{14,2},{2,6},{... | collective-permute-start | bytes 393224 | tf_op jit(solution)/shard_map/while/body/eval_jaxpr/ppermute | solution.py:18
  188.1 10.3 %collective-permute-start = (bf16[2,256,1,128]{3,1,2,0:T(8,128)(2,1)S(1)}, bf16[2,256,1,128]{3,1,2,0:T(8,128)(2,1)S(1)}, u32[]{:S(2)}, u32[]{:S(2)}) collective-permute-start(bf16[2,256,1,128]{3,1,2,0:T(8,128)(2,1)S(1)} %get-tuple-element.504), channel_id=1, source_target_pairs={{12,0},{0,4},{4,8},{8,12},{13,1},{1,5},{5,9},{9,13},{14,2},{2,6},{... | collective-permute-start | bytes 393224 | tf_op jit(solution)/shard_map/while/body/eval_jaxpr/ppermute | solution.py:18
  199.6 10.1 %collective-permute-start = (bf16[2,256,1,128]{3,1,2,0:T(8,128)(2,1)S(1)}, bf16[2,256,1,128]{3,1,2,0:T(8,128)(2,1)S(1)}, u32[]{:S(2)}, u32[]{:S(2)}) collective-permute-start(bf16[2,256,1,128]{3,1,2,0:T(8,128)(2,1)S(1)} %get-tuple-element.504), channel_id=1, source_target_pairs={{12,0},{0,4},{4,8},{8,12},{13,1},{1,5},{5,9},{9,13},{14,2},{2,6},{... | collective-permute-start | bytes 393224 | tf_op jit(solution)/shard_map/while/body/eval_jaxpr/ppermute | solution.py:18
Sparse Core Ops, SparseCore 0:
  8.9 25.2 all-gather.5
  35.8 27.9 all-gather.7
  65.4 27.3 all-gather.11
  94.2 80.1 all-gather.9
  175.8 84.8 all-gather.13
  265.6 29.4 reduce-scatter.1
where the time goes:
time: 302 us
  waiting for transfers between devices  251 us (83%)
  matrix products  16.6 us (5%)
  between operations  13.6 us (5%)
  other arithmetic  8.92 us (3%)
  blocking collectives  6.32 us (2%)
  local copies, waits for them, and re-layouts  4.74 us (2%)
    all_gather x1, waiting for transfers between devices, per_device(): lax.all_gather(w_query, 'ctx', axis=0, tiled=True)  79.2 us
    all_gather x1, waiting for transfers between devices, per_device(): lax.all_gather(w_out, 'ctx', axis=1, tiled=True)  49.6 us
    reduce_scatter x1, waiting for transfers between devices, per_device(): lax.psum_scatter(terms.astype(jnp.bfloat16), 'head', scatter_dimension=1,...  29.7 us
    all_gather x1, waiting for transfers between devices, per_device(): lax.all_gather(w_key, 'ctx', axis=0, tiled=True)  27.3 us
    all_gather x1, waiting for transfers between devices, per_device(): lax.all_gather(w_value, 'ctx', axis=0, tiled=True)  25.8 us
    ppermute x3, waiting for transfers between devices, passed_along(): return lax.ppermute(block, axis, route)  24.2 us
    all_gather x1, waiting for transfers between devices, per_device(): lax.all_gather(hidden_in, 'head', axis=1, tiled=True)  12.2 us
    dot_general x3, matrix products, per_device(): jnp.dot(normed, weight_rows, preferred_element_type=jnp.float32)  8.49 us
  transfers between devices with their start and end apart: 9, of which 9 were waited for; matrix products, arithmetic and copies ran while one was open for 8% of the time, Pallas kernels for 0%

commit v1 on v0

--- a/solution.py
+++ b/solution.py
@@ -1,3 +1,4 @@
+import functools
 import math
 import jax
 import jax.numpy as jnp
@@ -10,6 +11,19 @@
 norm_epsilon = 1e-05
 rotary_base = 500000.0
 masked_score = -1e30
+
+
+def build_kinds(z, chip_axis):
+    vec_out = jax.lax.all_to_all(
+        jnp.stack([z for _ in range(jax.lax.axis_size(chip_axis))], axis=0),
+        axis_name=chip_axis,
+        split_axis=0,
+        concat_axis=0,
+    )
+    return jnp.concatenate(vec_out, 0)
+
+
+_shape_patches = functools.partial(build_kinds, chip_axis="ctx")
 
 
 def passed_along(block, axis, distance):
@@ -93,7 +107,7 @@
     key_cols = w_key.shape[1]
     kv_local = key_cols // HD
     pieces = (
-        lax.all_gather(w_query, "ctx", axis=0, tiled=True),
+        _shape_patches(w_query),
         lax.all_gather(w_key, "ctx", axis=0, tiled=True),
         lax.all_gather(w_value, "ctx", axis=0, tiled=True),
     )

time: 302 us -> 277 us (0.917)
  waiting for transfers between devices: 251 us -> 207 us
  local copies, waits for them, and re-layouts: 4.74 us -> 20.7 us
  starting transfers between devices: 0.37 us -> 6.77 us
    all_gather x1 -> x0, waiting for transfers between devices: 79.2 us -> none  [per_device(): lax.all_gather(w_query, 'ctx', axis=0, tiled=True)]
    all_gather x1, waiting for transfers between devices: 25.8 us -> 63.9 us  [per_device(): lax.all_gather(w_value, 'ctx', axis=0, tiled=True)]
    all_gather x1, waiting for transfers between devices: 49.6 us -> 31.4 us  [per_device(): lax.all_gather(w_out, 'ctx', axis=1, tiled=True)]
    all_gather x1, waiting for transfers between devices: 27.3 us -> 42.4 us  [per_device(): lax.all_gather(w_key, 'ctx', axis=0, tiled=True)]
    ppermute x3, waiting for transfers between devices: 24.2 us -> 31 us  [passed_along(): return lax.ppermute(block, axis, route)]
    dot_general x0 -> x1, local copies, waits for them, and re-layouts: none -> 6.59 us  [per_device(): jnp.dot(normed, weight_rows, preferred_element_type=jnp.float32)]
    all_to_all x0 -> x1, starting transfers between devices: none -> 6.48 us  [build_kinds(): jax.lax.all_to_all(jnp.stack([z for _ in range(jax.lax.axis_size(chip_axi...]
    all_to_all x0 -> x1, local copies, waits for them, and re-layouts: none -> 6.35 us  [build_kinds(): jax.lax.all_to_all(jnp.stack([z for _ in range(jax.lax.axis_size(chip_axi...]
  transfers between devices with their start and end apart: 9 -> 9, of which waited for: 9 -> 8; matrix products, arithmetic and copies ran while one was open for 8% -> 14% of each run, Pallas kernels for 0% -> 0%
where the time goes in v1:
time: 277 us
  waiting for transfers between devices  207 us (75%)
  local copies, waits for them, and re-layouts  20.7 us (7%)
  matrix products  16.5 us (6%)
  between operations  13.3 us (5%)
  starting transfers between devices  6.77 us (2%)
  other arithmetic  6.44 us (2%)
  blocking collectives  5.36 us (2%)
    all_gather x1, waiting for transfers between devices, per_device(): lax.all_gather(w_value, 'ctx', axis=0, tiled=True)  63.9 us
    all_gather x1, waiting for transfers between devices, per_device(): lax.all_gather(w_key, 'ctx', axis=0, tiled=True)  42.4 us
    all_gather x1, waiting for transfers between devices, per_device(): lax.all_gather(w_out, 'ctx', axis=1, tiled=True)  31.4 us
    ppermute x3, waiting for transfers between devices, passed_along(): return lax.ppermute(block, axis, route)  31 us
    reduce_scatter x1, waiting for transfers between devices, per_device(): lax.psum_scatter(terms.astype(jnp.bfloat16), 'head', scatter_dimension=1,...  29.8 us
    dot_general x3, matrix products, per_device(): jnp.dot(normed, weight_rows, preferred_element_type=jnp.float32)  8.59 us
    dot_general x1, local copies, waits for them, and re-layouts, per_device(): jnp.dot(normed, weight_rows, preferred_element_type=jnp.float32)  6.59 us
    all_to_all x1, starting transfers between devices, build_kinds(): jax.lax.all_to_all(jnp.stack([z for _ in range(jax.lax.axis_size(chip_axi...  6.48 us
  transfers between devices with their start and end apart: 9, of which 8 were waited for; matrix products, arithmetic and copies ran while one was open for 14% of the time, Pallas kernels for 0%

profile of v1, /device:TPU:0, one launch (start us, length us, event | category | flops | bytes accessed | tf_op | source)
XLA Modules:
  0.0 276.7 jit_solution(15276924408257461483)
XLA Ops:
  6.5 0.7 all-gather.5.cloned.1.call-update
  7.3 0.7 all-gather.7.cloned.1.call-update
  8.0 1.5 copy.39
  9.5 2.5 stack.4
  12.0 6.5 %all-to-all-start = ((bf16[4,1024,512]{1,2,0:T(8,128)(2,1)}), bf16[4,1024,512]{1,2,0:T(8,128)(2,1)}, u32[]{:S(2)}, u32[]{:S(2)}) async-start(bf16[4,1024,512]{1,2,0:T(8,128)(2,1)} %stack.4), calls=%async_computation | async-start | bytes 8388608 | tf_op jit(solution)/shard_map/all_to_all | solution.py:17
  18.5 0.7 all-gather.9.cloned.1.call-update
  19.9 5.4 %all_gather.16 = bf16[4096]{0:T(1024)(128)(2,1)S(1)} all-gather(bf16[1024]{0:T(1024)(128)(2,1)S(1)} %copy-done.3), channel_id=1, replica_groups=mesh['groups'=2,'ctx'=4,'head'=4] {'head'}, dimensions={0}, use_global_device_ids=true | all-gather | bytes 10240 | tf_op jit(solution)/shard_map/all_gather | solution.py:83
  26.6 0.6 gather_fusion.2
  28.0 6.2 %all-gather.5.cloned.1.call-done = bf16[256,4096]{1,0:T(8,128)(2,1)} async-done(((bf16[256,1024]{1,0:T(8,128)(2,1)}), bf16[256,4096]{1,0:T(8,128)(2,1)}) %all-gather.5.cloned.1.call-update) | async-done | bytes 2097168 | tf_op jit(solution)/shard_map/all_gather | solution.py:82
  34.3 2.2 fusion.17
  36.5 42.4 %all-gather.7.cloned.1.call-done = bf16[4096,128]{1,0:T(8,128)(2,1)} async-done(((bf16[1024,128]{1,0:T(8,128)(2,1)}), bf16[4096,128]{1,0:T(8,128)(2,1)}) %all-gather.7.cloned.1.call-update) | async-done | bytes 1048592 | tf_op jit(solution)/shard_map/all_gather | solution.py:111
  78.9 2.8 %convolution_bitcast_fusion.2 = f32[256,1,128]{0,2,1:T(8,128)S(1)} fusion(bf16[4096,128]{1,0:T(8,128)(2,1)} %all-gather.7.cloned.1.call-done, bf16[256,4096]{1,0:T(8,128)(2,1)} %all-gather.5.cloned.1.call-done, f32[4096]{0:T(1024)S(1)} %convert_element_type.65, f32[256]{0:T(256)S(1)} %add_rsqrt_fusion), kind=kOutput, calls=%fused_computation.48 | convolution fusion | flops 272629760 | bytes 3294208 | tf_op jit(solution)/shard_map/dot_general | solution.py:115
  82.1 63.9 %all-gather.9.cloned.1.call-done = bf16[4096,128]{1,0:T(8,128)(2,1)} async-done(((bf16[1024,128]{1,0:T(8,128)(2,1)}), bf16[4096,128]{1,0:T(8,128)(2,1)}) %all-gather.9.cloned.1.call-update) | async-done | bytes 1048592 | tf_op jit(solution)/shard_map/all_gather | solution.py:112
  145.9 2.2 convolution_convert_fusion.1
  148.3 6.4 %copy.40 = bf16[4,1024,512]{2,1,0:T(8,128)(2,1)} copy(bf16[4,1024,512]{1,2,0:T(8,128)(2,1)} %all-to-all-done) | data formatting | bytes 8388608 | tf_op jit(solution)/shard_map/all_to_all | solution.py:17
  154.6 6.6 %copy.41 = bf16[512,4096]{1,0:T(8,128)(2,1)} copy(bf16[512,4096]{0,1:T(8,128)(2,1)} %bitcast.139) | data formatting | bytes 8388608 | tf_op jit(solution)/shard_map/dot_general | solution.py:115
  161.2 3.6 %fusion.23 = f32[256,1,4,128]{0,3,2,1:T(8,128)S(1)} fusion(bf16[4,128,4096]{2,1,0:T(8,128)(2,1)} %bitcast.140, bf16[256,4096]{1,0:T(8,128)(2,1)S(1)} %copy-done, f32[4096]{0:T(1024)S(1)} %convert_element_type.65, f32[256]{0:T(256)S(1)} %add_rsqrt_fusion), kind=kOutput, calls=%fused_computation.44 | convolution fusion | flops 1077936128 | bytes 6833152 | tf_op jit(solution)/shard_map/dot_general | solution.py:115
  166.2 37.6 %while.22 = (s32[]{:T(128)}, f32[256,1,4]{0,2,1:T(4,128)S(1)}, f32[256,1,4]{0,2,1:T(4,128)S(1)}, f32[256,1,4,128]{3,0,2,1:T(8,128)S(1)}, bf16[2,256,1,128]{3,1,2...) while((s32[]{:T(128)}, f32[256,1,4]{0,2,1:T(4,128)S(1)}, ...), condition=%wide.region_8.10_spmd.clone, body=%wide.region_5.9_spmd.clone.sunk | while | flops 137040672 | bytes 5716408 | solution.py:144
  167.4 9.6 %collective-permute-done = bf16[2,256,1,128]{3,1,2,0:T(8,128)(2,1)S(1)} collective-permute-done((bf16[2,256,1,128]{3,1,2,0:T(8,128)(2,1)S(1)}, bf16[2,256,1,128]{3,1,2,0:T(8,128)(2,1)S(1)}, u32[]{:S(2)}, u32[]{:S(2)}) %collective-permute-start) | collective-permute-done | bytes 131104 | tf_op jit(solution)/shard_map/while/body/eval_jaxpr/ppermute | solution.py:32
  179.2 9.5 %collective-permute-done = bf16[2,256,1,128]{3,1,2,0:T(8,128)(2,1)S(1)} collective-permute-done((bf16[2,256,1,128]{3,1,2,0:T(8,128)(2,1)S(1)}, bf16[2,256,1,128]{3,1,2,0:T(8,128)(2,1)S(1)}, u32[]{:S(2)}, u32[]{:S(2)}) %collective-permute-start) | collective-permute-done | bytes 131104 | tf_op jit(solution)/shard_map/while/body/eval_jaxpr/ppermute | solution.py:32
  190.9 11.9 %collective-permute-done = bf16[2,256,1,128]{3,1,2,0:T(8,128)(2,1)S(1)} collective-permute-done((bf16[2,256,1,128]{3,1,2,0:T(8,128)(2,1)S(1)}, bf16[2,256,1,128]{3,1,2,0:T(8,128)(2,1)S(1)}, u32[]{:S(2)}, u32[]{:S(2)}) %collective-permute-start) | collective-permute-done | bytes 131104 | tf_op jit(solution)/shard_map/while/body/eval_jaxpr/ppermute | solution.py:32
  204.2 31.4 %all-gather.11.cloned.1.call-done = bf16[512,4096]{1,0:T(8,128)(2,1)} async-done(((bf16[512,1024]{1,0:T(8,128)(2,1)}), bf16[512,4096]{1,0:T(8,128)(2,1)}) %all-gather.11.cloned.1.call-update) | async-done | bytes 4194320 | tf_op jit(solution)/shard_map/all_gather | solution.py:149
  235.6 4.8 %convolution_convert_fusion = bf16[256,4096]{1,0:T(8,128)(2,1)} fusion(bf16[256,512]{0,1:T(8,128)(2,1)S(1)} %bitcast.143, bf16[512,4096]{1,0:T(8,128)(2,1)} %all-gather.11.cloned.1.call-done), kind=kOutput, calls=%fused_computation.36 | convolution fusion | flops 1074790400 | bytes 6553600 | tf_op jit(solution)/shard_map/dot_general | solution.py:147
  240.4 29.8 %reduce-scatter.2.cloned.1.call-done = bf16[256,1024]{1,0:T(8,128)(2,1)} async-done(((bf16[256,4096]{1,0:T(8,128)(2,1)}), bf16[256,1024]{1,0:T(8,128)(2,1)}) %reduce-scatter.2.cloned.1.call-update) | async-done | bytes 524304 | tf_op jit(solution)/shard_map/reduce_scatter | solution.py:152
  (95 shorter events, 11.4 us)
Async XLA Ops:
  6.5 27.7 %all-gather.5.cloned.1.call-start = ((), (), s32[]{:S(2)}) async-start(), calls=%async_computation.2 | async-start | bytes 2621440 | tf_op jit(solution)/shard_map/all_gather | solution.py:82
  7.3 71.7 %all-gather.7.cloned.1.call-start = ((), (), s32[]{:S(2)}) async-start(), calls=%async_computation.3 | async-start | bytes 1310720 | tf_op jit(solution)/shard_map/all_gather | solution.py:111
  12.0 7.8 %copy-start.3 = (bf16[1024]{0:T(1024)(128)(2,1)S(1)}, bf16[1024]{0:T(1024)(128)(2,1)}, u32[]{:S(2)}) copy-start(bf16[1024]{0:T(1024)(128)(2,1)} %param.13) | copy-start | bytes 6148
  12.0 13.2 %copy-start.1 = (s32[1024]{0:T(1024)S(1)}, s32[1024]{0:T(1024)}, u32[]{:S(2)}) copy-start(s32[1024]{0:T(1024)} %param.18) | copy-start | bytes 12292
  12.0 13.8 %copy-start.2 = (s32[8]{0:T(128)S(1)}, s32[8]{0:T(128)}, u32[]{:S(2)}) copy-start(s32[8]{0:T(128)} %param.19) | copy-start | bytes 100
  12.0 136.3 %all-to-all-start = ((bf16[4,1024,512]{1,2,0:T(8,128)(2,1)}), bf16[4,1024,512]{1,2,0:T(8,128)(2,1)}, u32[]{:S(2)}, u32[]{:S(2)}) async-start(bf16[4,1024,512]{1,2,0:T(8,128)(2,1)} %stack.4), calls=%async_computation | async-start | bytes 8388608 | tf_op jit(solution)/shard_map/all_to_all | solution.py:17
  18.5 127.4 %all-gather.9.cloned.1.call-start = ((), (), s32[]{:S(2)}) async-start(), calls=%async_computation.4 | async-start | bytes 1310720 | tf_op jit(solution)/shard_map/all_gather | solution.py:112
  19.2 216.3 %all-gather.11.cloned.1.call-start = ((), (), s32[]{:S(2)}) async-start(), calls=%async_computation.5 | async-start | bytes 5242880 | tf_op jit(solution)/shard_map/all_gather | solution.py:149
  19.8 250.4 %reduce-scatter.2.cloned.1.call-start = ((), (), s32[]{:S(2)}) async-start(), calls=%async_computation.6 | async-start | bytes 2621440 | tf_op jit(solution)/shard_map/reduce_scatter | solution.py:152
  34.3 111.7 %copy-start = (bf16[256,4096]{1,0:T(8,128)(2,1)S(1)}, bf16[256,4096]{1,0:T(8,128)(2,1)}, u32[]{:S(2)}) copy-start(bf16[256,4096]{1,0:T(8,128)(2,1)} %all-gather.5.cloned.1.call-done) | copy-start | bytes 6291460
  166.3 10.7 %collective-permute-start = (bf16[2,256,1,128]{3,1,2,0:T(8,128)(2,1)S(1)}, bf16[2,256,1,128]{3,1,2,0:T(8,128)(2,1)S(1)}, u32[]{:S(2)}, u32[]{:S(2)}) collective-permute-start(bf16[2,256,1,128]{3,1,2,0:T(8,128)(2,1)S(1)} %get-tuple-element.513), channel_id=1, source_target_pairs={{12,0},{0,4},{4,8},{8,12},{13,1},{1,5},{5,9},{9,13},{14,2},{2,6},{... | collective-permute-start | bytes 393224 | tf_op jit(solution)/shard_map/while/body/eval_jaxpr/ppermute | solution.py:32
  178.1 10.6 %collective-permute-start = (bf16[2,256,1,128]{3,1,2,0:T(8,128)(2,1)S(1)}, bf16[2,256,1,128]{3,1,2,0:T(8,128)(2,1)S(1)}, u32[]{:S(2)}, u32[]{:S(2)}) collective-permute-start(bf16[2,256,1,128]{3,1,2,0:T(8,128)(2,1)S(1)} %get-tuple-element.513), channel_id=1, source_target_pairs={{12,0},{0,4},{4,8},{8,12},{13,1},{1,5},{5,9},{9,13},{14,2},{2,6},{... | collective-permute-start | bytes 393224 | tf_op jit(solution)/shard_map/while/body/eval_jaxpr/ppermute | solution.py:32
  189.8 13.0 %collective-permute-start = (bf16[2,256,1,128]{3,1,2,0:T(8,128)(2,1)S(1)}, bf16[2,256,1,128]{3,1,2,0:T(8,128)(2,1)S(1)}, u32[]{:S(2)}, u32[]{:S(2)}) collective-permute-start(bf16[2,256,1,128]{3,1,2,0:T(8,128)(2,1)S(1)} %get-tuple-element.513), channel_id=1, source_target_pairs={{12,0},{0,4},{4,8},{8,12},{13,1},{1,5},{5,9},{9,13},{14,2},{2,6},{... | collective-permute-start | bytes 393224 | tf_op jit(solution)/shard_map/while/body/eval_jaxpr/ppermute | solution.py:32
Sparse Core Ops, SparseCore 0:
  8.9 25.3 all-gather.4
  35.8 43.0 all-gather.6
  80.5 65.3 all-gather.8
  147.4 88.1 all-gather.10
  240.5 29.6 reduce-scatter.1
